TPU v7x, 256 devices: a whole 4x4x8 slice. The times are simulated.
256 devices in a mesh: gy: 8 (over y, x_hi), gx: 4 (over x_lo, core), wa: 8 (over z).
Axes of the slice: x: 4 (x_hi: 2, x_lo: 2; x = x_hi * 2 + x_lo), y: 4, z: 8, core: 2. Of those that a mesh axis runs over, the one named last changes fastest.
Arguments:
- tokens: bfloat16 [8, 64, 128, 3072], P('wa', 'gy', 'gx'), may hold values from -6 to 6
- mod_shift: float32 [8, 3072], P('wa'), may hold values from -3 to 3
- mod_scale: float32 [8, 3072], P('wa'), may hold values from -0.9 to 3.9
- qkv_weight: bfloat16 [3072, 4608], P(None, ('gx', 'wa')), may hold values from -0.14433757 to 0.14433757
- block_codes: int32 [8, 16, 9], P('gy', 'gx'), may hold values from 0 to 8, as said below
- block_counts: int32 [8, 16], P('gy', 'gx'), may hold values from 1 to 9, as said below
- valid_tokens: int32 [8, 16], replicated, may hold values from 1 to 64
Outputs:
- attended: bfloat16 [8, 64, 128, 1536], P('wa', 'gy', 'gx')
Inputs may be any that keep to these rules, and one draw needn't show every extreme that they name: `block_codes`: the 9 codes of a block's list are distinct, the first is 4 (the block itself), and the first block_counts entries name blocks inside the grid. `block_counts`: A count never exceeds the number of blocks of the 3 x 3 neighbourhood that lie inside the grid.
All inputs are finite; a program needn't handle non-finite values.
Results may differ from a plain program's by a relative error of at most 0.007.
Values may be sent and summed in bfloat16 or wider, within the bound.
No kernel may reach another device: no remote copies, remote signals or barrier semaphores. Data moves between devices by JAX's collectives and lax.ppermute only.
A program may use at most 128 MiB of HBM per device.

v0:
```python
import math
import jax
import jax.numpy as jnp
from jax import lax
from jax.sharding import PartitionSpec as P

D = 3072
HEADS = 12
HD = 128
BLK = 8
NBR = 9


def extended_2(array, sides, width):
    for axis, dim in sides:
        size, length = (lax.axis_size(axis), array.shape[dim])
        up = [(i, (i + 1) % size) for i in range(size - 1)]
        down = [(j, i) for i, j in up]
        last = lax.slice_in_dim(array, length - width, length, axis=dim)
        first = lax.slice_in_dim(array, 0, width, axis=dim)
        before = lax.ppermute(last, axis, up)
        after = lax.ppermute(first, axis, down)
        array = jnp.concatenate([before, array, after], axis=dim)
    return array


def normalize(rows, shift_row, scale_row):
    widened = rows.astype(jnp.float32)
    average = jnp.mean(widened, axis=-1, keepdims=True)
    centred = widened - average
    spread = jnp.mean(centred * centred, axis=-1, keepdims=True)
    return (centred * lax.rsqrt(spread + 1e-06) * (1.0 + scale_row) + shift_row).astype(
        jnp.bfloat16
    )


def to_blocks(field):
    height, breadth, channels = field.shape
    shaped = field.reshape(height // BLK, BLK, breadth // BLK, BLK, channels)
    return shaped.transpose(0, 2, 1, 3, 4).reshape(
        height // BLK, breadth // BLK, BLK * BLK, channels
    )


def from_blocks(blocks):
    block_rows, block_cols, cells, channels = blocks.shape
    shaped = blocks.reshape(block_rows, block_cols, BLK, BLK, channels)
    return shaped.transpose(0, 2, 1, 3, 4).reshape(block_rows * BLK, block_cols * BLK, channels)


def make_mask(counts, live_count):
    slot_ids = jnp.arange(NBR, dtype=jnp.int32)
    token_ids = jnp.arange(BLK * BLK, dtype=jnp.int32)
    used = slot_ids[:, None] < counts[..., None, None]
    return used & (token_ids < live_count[..., None])


def attend(queries, key_blocks, key_mask):
    number = queries.shape[0]
    query_heads = queries.reshape(number, BLK * BLK, HEADS, HD)
    key_value = key_blocks.reshape(number, NBR * BLK * BLK, 2, HEADS, HD)
    scores = jnp.einsum(
        "nqhd,nkhd->nhqk", query_heads, key_value[:, :, 0], preferred_element_type=jnp.float32
    ) * (1.0 / math.sqrt(HD))
    scores = jnp.where(key_mask[:, None, None, :], scores, -jnp.inf)
    highest = jnp.max(scores, axis=-1, keepdims=True)
    exponent = jnp.exp(scores - highest)
    probs = (exponent / jnp.sum(exponent, axis=-1, keepdims=True)).astype(jnp.bfloat16)
    blended = jnp.einsum(
        "nhqk,nkhd->nqhd", probs, key_value[:, :, 1], preferred_element_type=jnp.float32
    )
    return blended.astype(jnp.bfloat16).reshape(number, BLK * BLK, HEADS * HD)


def body(tokens, mod_shift, mod_scale, qkv_weight, block_codes, block_counts, valid_tokens):
    tile_rows = tokens.shape[1]
    tile_cols = tokens.shape[2]
    width = HEADS * HD
    flat_rows = normalize(tokens[0], mod_shift[0], mod_scale[0]).reshape(tile_rows * tile_cols, D)
    qkv = jnp.dot(
        flat_rows,
        lax.all_gather(qkv_weight, ("gx", "wa"), axis=1, tiled=True),
        preferred_element_type=jnp.float32,
    ).astype(jnp.bfloat16)
    qkv_grid = qkv.reshape(tile_rows, tile_cols, 3 * width)
    extended = extended_2(qkv_grid[:, :, width:], (("gy", 0), ("gx", 1)), BLK)
    block_rows = tile_rows // BLK
    block_cols = tile_cols // BLK
    queries = to_blocks(qkv_grid[:, :, :width])
    key_blocks = to_blocks(extended)
    row_ids = jnp.arange(block_rows, dtype=jnp.int32)[:, None, None]
    col_ids = jnp.arange(block_cols, dtype=jnp.int32)[None, :, None]
    row_step = block_codes // 3 - 1
    col_step = block_codes % 3 - 1
    picked = key_blocks[row_ids + 1 + row_step, col_ids + 1 + col_step]
    global_row = jnp.clip(
        lax.axis_index("gy") * block_rows + row_ids + row_step, 0, valid_tokens.shape[0] - 1
    )
    global_col = jnp.clip(
        lax.axis_index("gx") * block_cols + col_ids + col_step, 0, valid_tokens.shape[1] - 1
    )
    live_count = valid_tokens[global_row, global_col]
    key_mask = make_mask(block_counts, live_count)
    number = block_rows * block_cols
    result = attend(
        queries.reshape(number, BLK * BLK, width),
        picked.reshape(number, NBR, BLK * BLK, 2 * width),
        key_mask.reshape(number, NBR * BLK * BLK),
    )
    return from_blocks(result.reshape(block_rows, block_cols, BLK * BLK, width))[None]


def solution(mesh):
    return jax.shard_map(
        body,
        mesh=mesh,
        in_specs=(
            P("wa", "gy", "gx", None),
            P("wa", None),
            P("wa", None),
            P(None, ("gx", "wa")),
            P("gy", "gx", None),
            P("gy", "gx"),
            P(),
        ),
        out_specs=P("wa", "gy", "gx", None),
        check_vma=False,
    )
```

profile of v0, /device:TPU:29, one launch (start us, length us, event | category | flops | bytes accessed | tf_op | source)
XLA Modules:
  0.0 368.1 jit_solution(4767164489304758296)
XLA Ops:
  7.3 1.7 convert_reduce_fusion
  9.1 2.0 fusion.8
  12.0 162.2 %all-gather.2.cloned.1.call-done = bf16[3072,4608]{0,1:T(8,128)(2,1)} async-done(((bf16[3072,144]{0,1:T(8,128)(2,1)}), bf16[3072,4608]{0,1:T(8,128)(2,1)}) %all-gather.2.cloned.1.call-update) | async-done | bytes 28311568 | tf_op jit(solution)/shard_map/all_gather | solution.py:82
  174.2 13.0 %convolution_convert_fusion = bf16[256,4608]{1,0:T(8,128)(2,1)S(1)} fusion(bf16[256,3072]{1,0:T(8,128)(2,1)S(1)} %fusion.12, bf16[3072,4608]{0,1:T(8,128)(2,1)} %all-gather.2.cloned.1.call-done), kind=kOutput, calls=%fused_computation.12 | convolution fusion | flops 7248936960 | bytes 32243712 | tf_op jit(solution)/shard_map/dot_general | solution.py:80
  187.4 1.2 copy-done.4
  188.6 2.4 collective-permute-start.1
  191.0 1.3 collective-permute-start
  192.5 31.9 %collective-permute-done.1 = bf16[8,32,3072]{2,1,0:T(8,128)(2,1)S(1)} collective-permute-done((bf16[8,32,3072]{2,1,0:T(8,128)(2,1)S(1)}, bf16[8,32,3072]{2,1,0:T(8,128)(2,1)S(1)}, u32[]{:S(2)}, u32[]{:S(2)}) %collective-permute-start.1) | collective-permute-done | bytes 1572896 | tf_op jit(solution)/shard_map/ppermute | solution.py:22
  224.4 37.2 %collective-permute-done = bf16[8,32,3072]{2,1,0:T(8,128)(2,1)} collective-permute-done((bf16[8,32,3072]{2,1,0:T(8,128)(2,1)S(1)}, bf16[8,32,3072]{2,1,0:T(8,128)(2,1)}, u32[]{:S(2)}, u32[]{:S(2)}) %collective-permute-start) | collective-permute-done | bytes 1572896 | tf_op jit(solution)/shard_map/ppermute | solution.py:21
  261.6 2.8 pad_maximum_fusion.3
  264.4 4.1 %collective-permute-start.2 = (bf16[24,8,3072]{2,1,0:T(8,128)(2,1)}, bf16[24,8,3072]{2,1,0:T(8,128)(2,1)}, u32[]{:S(2)}, u32[]{:S(2)}) collective-permute-start(bf16[24,8,3072]{2,1,0:T(8,128)(2,1)} %get-tuple-element.7), channel_id=1, source_target_pairs={{0,8},{8,16},{16,24},{1,9},{9,17},{17,25},{2,10},{10,18},{18,26},{... | collective-permute-start | bytes 3538952 | tf_op jit(solution)/shard_map/ppermute | solution.py:21
  268.5 2.1 collective-permute-start.3
  272.2 1.2 slice_bitcast_fusion
  274.4 2.4 reshape_reshape_reshape.6
  276.7 5.2 %collective-permute-done.2 = bf16[24,8,3072]{2,1,0:T(8,128)(2,1)} collective-permute-done((bf16[24,8,3072]{2,1,0:T(8,128)(2,1)}, bf16[24,8,3072]{2,1,0:T(8,128)(2,1)}, u32[]{:S(2)}, u32[]{:S(2)}) %collective-permute-start.2) | collective-permute-done | bytes 1179680 | tf_op jit(solution)/shard_map/ppermute | solution.py:21
  281.9 4.4 %collective-permute-done.3 = bf16[24,8,3072]{2,1,0:T(8,128)(2,1)} collective-permute-done((bf16[24,8,3072]{2,1,0:T(8,128)(2,1)}, bf16[24,8,3072]{2,1,0:T(8,128)(2,1)}, u32[]{:S(2)}, u32[]{:S(2)}) %collective-permute-start.3) | collective-permute-done | bytes 1179680 | tf_op jit(solution)/shard_map/ppermute | solution.py:22
  286.3 3.3 pad_maximum_fusion
  289.6 3.7 %copy.33 = bf16[3,6,8,8,3072]{4,3,2,1,0:T(8,128)(2,1)} copy(bf16[3,6,8,8,3072]{4,3,1,2,0:T(8,128)(2,1)S(1)} %bitcast.68) | data formatting | bytes 14155776 | tf_op jit(solution)/shard_map/transpose | solution.py:40
  293.4 10.5 %gather_fusion = bf16[36,64,3072]{2,1,0:T(8,128)(2,1)} fusion(bf16[3,6,64,3072]{3,2,1,0:T(8,128)(2,1)} %bitcast.67, s32[36]{0:T(128)S(1)} %reshape.132), kind=kCustom, calls=%fused_computation | custom fusion | bytes 28311840 | tf_op jit(solution)/shard_map/gather | solution.py:95
  303.9 25.4 %reshape_reshape.3 = bf16[4,576,2,12,128]{4,3,2,1,0:T(8,128)(2,1)} reshape(bf16[36,64,3072]{2,1,0:T(8,128)(2,1)} %gather_fusion) | data formatting | bytes 28311552 | tf_op jit(solution)/shard_map/reshape;reshape | solution.py:61
  329.3 12.5 %fusion.30 = (bf16[4,576,1,12,128]{4,3,2,1,0:T(8,128)(2,1)S(1)}, bf16[4,576,1,12,128]{4,3,2,1,0:T(8,128)(2,1)}) fusion(bf16[4,576,2,12,128]{4,3,2,1,0:T(8,128)(2,1)} %reshape_reshape.3), kind=kLoop, calls=%fused_computation.69 | loop fusion | bytes 28311552 | tf_op jit(solution)/shard_map/slice | solution.py:63
  341.8 3.4 fusion.2
  345.2 4.4 %fusion.31 = (f32[4,12,64]{2,1,0:T(8,128)S(1)}, f32[4,12,64,576]{3,2,1,0:T(8,128)}) fusion(f32[4,12,64,576]{3,2,1,0:T(8,128)S(1)} %fusion.2, pred[4,576]{1,0:T(4,128)(4,1)S(1)} %compare_and_fusion), kind=kOutput, calls=%fused_computation.70 | output fusion | flops 10617407 | bytes 14170368 | tf_op jit(solution)/shard_map/sub | solution.py:67
  349.7 9.6 %fusion.14 = bf16[4,64,12,128]{3,1,2,0:T(8,128)(2,1)S(1)} fusion(bf16[4,576,1,12,128]{4,3,2,1,0:T(8,128)(2,1)} %get-tuple-element.6, f32[4,12,64,576]{3,2,1,0:T(8,128)} %get-tuple-element.14, f32[4,12,64]{2,1,0:T(8,128)S(1)} %get-tuple-element.13), kind=kOutput, calls=%fused_computation.27 | convolution fusion | flops 456916992 | bytes 14954496 | tf_op jit(solution)/shard_map/nhqk,nkhd->nqhd/dot_general | solution.py:69
  (48 shorter events, 6.6 us)
Async XLA Ops:
  6.5 264.1 %copy-start = (s32[8,16]{1,0:T(8,128)S(1)}, s32[8,16]{1,0:T(8,128)}, u32[]{:S(2)}) copy-start(s32[8,16]{1,0:T(8,128)} %param.13) | copy-start | bytes 1540
  6.5 4.6 %copy-start.2 = (bf16[1,8,32,3072]{3,2,1,0:T(8,128)(2,1)S(1)}, bf16[1,8,32,3072]{3,2,1,0:T(8,128)(2,1)}, u32[]{:S(2)}) copy-start(bf16[1,8,32,3072]{3,2,1,0:T(8,128)(2,1)} %param.7) | copy-start | bytes 4718596
  6.5 4.6 %copy-start.6 = (f32[1,3072]{1,0:T(1,128)S(1)}, f32[1,3072]{1,0:T(1,128)}, u32[]{:S(2)}) copy-start(f32[1,3072]{1,0:T(1,128)} %param.9) | copy-start | bytes 36868
  6.5 4.6 %copy-start.5 = (f32[1,3072]{1,0:T(1,128)S(1)}, f32[1,3072]{1,0:T(1,128)}, u32[]{:S(2)}) copy-start(f32[1,3072]{1,0:T(1,128)} %param.8) | copy-start | bytes 36868
  6.5 167.6 %all-gather.2.cloned.1.call-start = ((), (), s32[]{:S(2)}) async-start(), calls=%async_computation | async-start | bytes 29196288 | tf_op jit(solution)/shard_map/all_gather | solution.py:82
  12.0 180.4 %copy-start.7 = (s32[1,4,9]{2,1,0:T(4,128)S(1)}, s32[1,4,9]{2,1,0:T(4,128)}, u32[]{:S(2)}) copy-start(s32[1,4,9]{2,1,0:T(4,128)} %param.11) | copy-start | bytes 436
  187.2 1.4 copy-start.4
  188.6 35.8 %collective-permute-start.1 = (bf16[8,32,3072]{2,1,0:T(8,128)(2,1)S(1)}, bf16[8,32,3072]{2,1,0:T(8,128)(2,1)S(1)}, u32[]{:S(2)}, u32[]{:S(2)}) collective-permute-start(bf16[8,32,3072]{2,1,0:T(8,128)(2,1)S(1)} %slice.31), channel_id=1, source_target_pairs={{32,0},{64,32},{96,64},{128,96},{160,128},{192,160},{224,192},{33,... | collective-permute-start | bytes 4718600 | tf_op jit(solution)/shard_map/ppermute | solution.py:22
  191.0 70.6 %collective-permute-start = (bf16[8,32,3072]{2,1,0:T(8,128)(2,1)S(1)}, bf16[8,32,3072]{2,1,0:T(8,128)(2,1)}, u32[]{:S(2)}, u32[]{:S(2)}) collective-permute-start(bf16[8,32,3072]{2,1,0:T(8,128)(2,1)S(1)} %slice.31), channel_id=1, source_target_pairs={{0,32},{32,64},{64,96},{96,128},{128,160},{160,192},{192,224},{1,3... | collective-permute-start | bytes 4718600 | tf_op jit(solution)/shard_map/ppermute | solution.py:21
  192.4 79.3 %copy-start.8 = (s32[1,4]{1,0:T(1,128)S(1)}, s32[1,4]{1,0:T(1,128)}, u32[]{:S(2)}) copy-start(s32[1,4]{1,0:T(1,128)} %param.12) | copy-start | bytes 52
  264.4 17.5 %collective-permute-start.2 = (bf16[24,8,3072]{2,1,0:T(8,128)(2,1)}, bf16[24,8,3072]{2,1,0:T(8,128)(2,1)}, u32[]{:S(2)}, u32[]{:S(2)}) collective-permute-start(bf16[24,8,3072]{2,1,0:T(8,128)(2,1)} %get-tuple-element.7), channel_id=1, source_target_pairs={{0,8},{8,16},{16,24},{1,9},{9,17},{17,25},{2,10},{10,18},{18,26},{... | collective-permute-start | bytes 3538952 | tf_op jit(solution)/shard_map/ppermute | solution.py:21
  268.5 17.8 %collective-permute-start.3 = (bf16[24,8,3072]{2,1,0:T(8,128)(2,1)}, bf16[24,8,3072]{2,1,0:T(8,128)(2,1)}, u32[]{:S(2)}, u32[]{:S(2)}) collective-permute-start(bf16[24,8,3072]{2,1,0:T(8,128)(2,1)} %get-tuple-element.8), channel_id=1, source_target_pairs={{8,0},{16,8},{24,16},{9,1},{17,9},{25,17},{10,2},{18,10},{26,18},{... | collective-permute-start | bytes 3538952 | tf_op jit(solution)/shard_map/ppermute | solution.py:22
  329.3 12.5 %copy-start.3 = (bf16[4,64,12,128]{3,2,1,0:T(8,128)(2,1)S(1)}, bf16[4,64,12,128]{3,2,1,0:T(8,128)(2,1)}, u32[]{:S(2)}) copy-start(bf16[4,64,12,128]{3,2,1,0:T(8,128)(2,1)} %reshape_reshape_reshape.6) | copy-start | bytes 2359300
  349.7 11.6 %copy-start.1 = (s32[8,16]{1,0:T(8,128)S(1)}, s32[8,16]{1,0:T(8,128)}, u32[]{:S(2)}) copy-start(s32[8,16]{1,0:T(8,128)} %param.13) | copy-start | bytes 1540
Sparse Core Ops, SparseCore 0:
  9.2 164.9 all-gather.1
where the time goes:
time: 369 us; the launch traced here: 368 us
  waiting for transfers between devices  242 us (66%)
  local copies, waits for them, and re-layouts  61.8 us (17%)
  matrix products  26 us (7%)
  other arithmetic  15.2 us (4%)
  between operations  13.6 us (4%)
  starting transfers between devices  9.95 us (3%)
    all_gather x1, waiting for transfers between devices, body(): lax.all_gather(qkv_weight, ('gx', 'wa'), axis=1, tiled=True)  162 us
    ppermute x2, waiting for transfers between devices, extended_2(): before = lax.ppermute(last, axis, up)  42.4 us
    ppermute x2, waiting for transfers between devices, extended_2(): after = lax.ppermute(first, axis, down)  36.3 us
    another operation x1, local copies, waits for them, and re-layouts, attend(): key_value = key_blocks.reshape(number, NBR * BLK * BLK, 2, HEADS, HD)  25.4 us
    dot_general x1, matrix products, body(): jnp.dot(flat_rows, lax.all_gather(qkv_weight, ('gx', 'wa'), axis=1, tiled...  13 us
    slice x1, local copies, waits for them, and re-layouts, attend(): key_value[:, :, 0]  12.5 us
    gather x1, local copies, waits for them, and re-layouts, body(): picked = key_blocks[row_ids + 1 + row_step, col_ids + 1 + col_step]  10.5 us
    dot_general x1, matrix products, attend(): jnp.einsum('nhqk,nkhd->nqhd', probs, key_value[:, :, 1], preferred_elemen...  9.59 us
  transfers between devices with their start and end apart: 5, of which 5 were waited for; matrix products, arithmetic and copies ran while one was open for 3% of the time, Pallas kernels for 0%

commit v1 on v0

--- a/solution.py
+++ b/solution.py
@@ -77,11 +77,21 @@
     tile_cols = tokens.shape[2]
     width = HEADS * HD
     flat_rows = normalize(tokens[0], mod_shift[0], mod_scale[0]).reshape(tile_rows * tile_cols, D)
-    qkv = jnp.dot(
-        flat_rows,
-        lax.all_gather(qkv_weight, ("gx", "wa"), axis=1, tiled=True),
-        preferred_element_type=jnp.float32,
-    ).astype(jnp.bfloat16)
+
+    def find_yards(my_data):
+        return jnp.concatenate(
+            lax.all_to_all(
+                jnp.stack([my_data] * lax.psum(1, axis_name=("gx", "wa")), axis=0),
+                axis_name=("gx", "wa"),
+                split_axis=0,
+                concat_axis=0,
+            ),
+            axis=1,
+        )
+
+    qkv = jnp.dot(flat_rows, find_yards(qkv_weight), preferred_element_type=jnp.float32).astype(
+        jnp.bfloat16
+    )
     qkv_grid = qkv.reshape(tile_rows, tile_cols, 3 * width)
     extended = extended_2(qkv_grid[:, :, width:], (("gy", 0), ("gx", 1)), BLK)
     block_rows = tile_rows // BLK

time: 369 us -> 843 us (2.28)
  the two profiles are of different devices: /device:TPU:29 before, /device:TPU:105 now
where the time goes in v1:
time: 843 us; the launch traced here: 842 us
  waiting for transfers between devices  706 us (84%)
  local copies, waits for them, and re-layouts  72.1 us (9%)
  matrix products  26 us (3%)
  starting transfers between devices  25.3 us (3%)
  other arithmetic  12.5 us (1%)
    all_to_all x1, waiting for transfers between devices, find_yards(): lax.all_to_all(jnp.stack([my_data] * lax.psum(1, axis_name=('gx', 'wa')),...  631 us
    ppermute x2, waiting for transfers between devices, extended_2(): after = lax.ppermute(first, axis, down)  38.3 us
    ppermute x2, waiting for transfers between devices, extended_2(): before = lax.ppermute(last, axis, up)  36 us
    another operation x1, local copies, waits for them, and re-layouts, attend(): key_value = key_blocks.reshape(number, NBR * BLK * BLK, 2, HEADS, HD)  25.4 us
  transfers between devices with their start and end apart: 5, of which 5 were waited for; matrix products, arithmetic and copies ran while one was open for 1% of the time, Pallas kernels for 0%

profile of v1, /device:TPU:105, one launch (start us, length us, event | category | flops | bytes accessed | tf_op | source)
XLA Modules:
  0.0 841.6 jit_solution(1359951872132075497)
XLA Ops:
  0.0 10.4 %stack.2 = bf16[32,3072,144]{1,2,0:T(8,128)(2,1)} broadcast(bf16[3072,144]{0,1:T(8,128)(2,1)} %param.10), dimensions={1,2} | broadcast | bytes 29196288 | tf_op jit(solution)/shard_map/stack | solution.py:84
  10.4 9.2 %all-to-all-start = ((bf16[32,3072,144]{1,2,0:T(8,128)(2,1)}), bf16[32,3072,144]{1,2,0:T(8,128)(2,1)}, u32[]{:S(2)}, u32[]{:S(2)}) async-start(bf16[32,3072,144]{1,2,0:T(8,128)(2,1)} %stack.2), calls=%async_computation | async-start | bytes 56623104 | tf_op jit(solution)/shard_map/all_to_all | solution.py:83
  21.3 631.2 %all-to-all-done = bf16[32,3072,144]{1,2,0:T(8,128)(2,1)} async-done(((bf16[32,3072,144]{1,2,0:T(8,128)(2,1)}), bf16[32,3072,144]{1,2,0:T(8,128)(2,1)}, u32[]{:S(2)}, u32[]{:S(2)}) %all-to-all-start) | async-done | bytes 28311584 | tf_op jit(solution)/shard_map/all_to_all | solution.py:83
  652.5 13.0 %convolution_convert_fusion = bf16[256,4608]{1,0:T(8,128)(2,1)S(1)} fusion(bf16[256,3072]{1,0:T(8,128)(2,1)S(1)} %bitcast.67, bf16[3072,4608]{0,1:T(8,128)(2,1)} %bitcast.5), kind=kOutput, calls=%fused_computation.12 | convolution fusion | flops 7248936960 | bytes 32243712 | tf_op jit(solution)/shard_map/dot_general | solution.py:92
  665.8 1.2 copy-done.4
  667.0 4.3 collective-permute-start
  671.4 3.3 collective-permute-start.1
  674.8 30.9 %collective-permute-done = bf16[8,32,3072]{2,1,0:T(8,128)(2,1)S(1)} collective-permute-done((bf16[8,32,3072]{2,1,0:T(8,128)(2,1)S(1)}, bf16[8,32,3072]{2,1,0:T(8,128)(2,1)S(1)}, u32[]{:S(2)}, u32[]{:S(2)}) %collective-permute-start) | collective-permute-done | bytes 1572896 | tf_op jit(solution)/shard_map/ppermute | solution.py:21
  705.7 33.9 %collective-permute-done.1 = bf16[8,32,3072]{2,1,0:T(8,128)(2,1)} collective-permute-done((bf16[8,32,3072]{2,1,0:T(8,128)(2,1)S(1)}, bf16[8,32,3072]{2,1,0:T(8,128)(2,1)}, u32[]{:S(2)}, u32[]{:S(2)}) %collective-permute-start.1) | collective-permute-done | bytes 1572896 | tf_op jit(solution)/shard_map/ppermute | solution.py:22
  739.6 2.9 pad_maximum_fusion.3
  742.5 6.3 collective-permute-start.2
  748.8 2.1 collective-permute-start.3
  752.5 1.2 slice_bitcast_fusion
  754.7 2.4 reshape_reshape_reshape.6
  757.0 5.2 collective-permute-done.2
  762.2 4.4 collective-permute-done.3
  766.6 3.3 pad_maximum_fusion
  769.9 3.7 copy.34
  773.6 10.6 %gather_fusion = bf16[36,64,3072]{2,1,0:T(8,128)(2,1)} fusion(bf16[3,6,64,3072]{3,2,1,0:T(8,128)(2,1)} %bitcast.63, s32[36]{0:T(128)S(1)} %reshape.155), kind=kCustom, calls=%fused_computation | custom fusion | bytes 28311840 | tf_op jit(solution)/shard_map/gather | solution.py:105
  784.2 25.4 %reshape_reshape.3 = bf16[4,576,2,12,128]{4,3,2,1,0:T(8,128)(2,1)} reshape(bf16[36,64,3072]{2,1,0:T(8,128)(2,1)} %gather_fusion) | data formatting | bytes 28311552 | tf_op jit(solution)/shard_map/reshape;reshape | solution.py:61
  809.6 12.5 %fusion.31 = (bf16[4,576,1,12,128]{4,3,2,1,0:T(8,128)(2,1)S(1)}, bf16[4,576,1,12,128]{4,3,2,1,0:T(8,128)(2,1)}) fusion(bf16[4,576,2,12,128]{4,3,2,1,0:T(8,128)(2,1)} %reshape_reshape.3), kind=kLoop, calls=%fused_computation.70 | loop fusion | bytes 28311552 | tf_op jit(solution)/shard_map/slice | solution.py:63
  822.2 3.4 fusion.2
  825.6 4.4 fusion.32
  830.0 9.6 %fusion.15 = bf16[4,64,12,128]{3,1,2,0:T(8,128)(2,1)S(1)} fusion(bf16[4,576,1,12,128]{4,3,2,1,0:T(8,128)(2,1)} %get-tuple-element.6, f32[4,12,64,576]{3,2,1,0:T(8,128)} %get-tuple-element.14, f32[4,12,64]{2,1,0:T(8,128)S(1)} %get-tuple-element.13), kind=kOutput, calls=%fused_computation.28 | convolution fusion | flops 456916992 | bytes 14954496 | tf_op jit(solution)/shard_map/nhqk,nkhd->nqhd/dot_general | solution.py:69
  (46 shorter events, 6.6 us)
Async XLA Ops:
  0.0 751.1 %copy-start = (s32[8,16]{1,0:T(8,128)S(1)}, s32[8,16]{1,0:T(8,128)}, u32[]{:S(2)}) copy-start(s32[8,16]{1,0:T(8,128)} %param.13) | copy-start | bytes 1540
  10.4 9.2 %copy-start.2 = (bf16[1,8,32,3072]{3,2,1,0:T(8,128)(2,1)S(1)}, bf16[1,8,32,3072]{3,2,1,0:T(8,128)(2,1)}, u32[]{:S(2)}) copy-start(bf16[1,8,32,3072]{3,2,1,0:T(8,128)(2,1)} %param.7) | copy-start | bytes 4718596
  10.4 10.1 %copy-start.6 = (f32[1,3072]{1,0:T(1,128)S(1)}, f32[1,3072]{1,0:T(1,128)}, u32[]{:S(2)}) copy-start(f32[1,3072]{1,0:T(1,128)} %param.9) | copy-start | bytes 36868
  10.4 10.1 %copy-start.5 = (f32[1,3072]{1,0:T(1,128)S(1)}, f32[1,3072]{1,0:T(1,128)}, u32[]{:S(2)}) copy-start(f32[1,3072]{1,0:T(1,128)} %param.8) | copy-start | bytes 36868
  10.4 642.1 %all-to-all-start = ((bf16[32,3072,144]{1,2,0:T(8,128)(2,1)}), bf16[32,3072,144]{1,2,0:T(8,128)(2,1)}, u32[]{:S(2)}, u32[]{:S(2)}) async-start(bf16[32,3072,144]{1,2,0:T(8,128)(2,1)} %stack.2), calls=%async_computation | async-start | bytes 56623104 | tf_op jit(solution)/shard_map/all_to_all | solution.py:83
  652.5 22.2 %copy-start.7 = (s32[1,4,9]{2,1,0:T(4,128)S(1)}, s32[1,4,9]{2,1,0:T(4,128)}, u32[]{:S(2)}) copy-start(s32[1,4,9]{2,1,0:T(4,128)} %param.11) | copy-start | bytes 436
  665.6 1.4 copy-start.4
  667.0 38.7 %collective-permute-start = (bf16[8,32,3072]{2,1,0:T(8,128)(2,1)S(1)}, bf16[8,32,3072]{2,1,0:T(8,128)(2,1)S(1)}, u32[]{:S(2)}, u32[]{:S(2)}) collective-permute-start(bf16[8,32,3072]{2,1,0:T(8,128)(2,1)S(1)} %slice.31), channel_id=1, source_target_pairs={{0,32},{32,64},{64,96},{96,128},{128,160},{160,192},{192,224},{1,3... | collective-permute-start | bytes 4718600 | tf_op jit(solution)/shard_map/ppermute | solution.py:21
  671.4 68.3 %collective-permute-start.1 = (bf16[8,32,3072]{2,1,0:T(8,128)(2,1)S(1)}, bf16[8,32,3072]{2,1,0:T(8,128)(2,1)}, u32[]{:S(2)}, u32[]{:S(2)}) collective-permute-start(bf16[8,32,3072]{2,1,0:T(8,128)(2,1)S(1)} %slice.31), channel_id=1, source_target_pairs={{32,0},{64,32},{96,64},{128,96},{160,128},{192,160},{224,192},{33,... | collective-permute-start | bytes 4718600 | tf_op jit(solution)/shard_map/ppermute | solution.py:22
  674.8 77.4 %copy-start.8 = (s32[1,4]{1,0:T(1,128)S(1)}, s32[1,4]{1,0:T(1,128)}, u32[]{:S(2)}) copy-start(s32[1,4]{1,0:T(1,128)} %param.12) | copy-start | bytes 52
  742.5 19.7 %collective-permute-start.2 = (bf16[24,8,3072]{2,1,0:T(8,128)(2,1)}, bf16[24,8,3072]{2,1,0:T(8,128)(2,1)}, u32[]{:S(2)}, u32[]{:S(2)}) collective-permute-start(bf16[24,8,3072]{2,1,0:T(8,128)(2,1)} %get-tuple-element.7), channel_id=1, source_target_pairs={{0,8},{8,16},{16,24},{1,9},{9,17},{17,25},{2,10},{10,18},{18,26},{... | collective-permute-start | bytes 3538952 | tf_op jit(solution)/shard_map/ppermute | solution.py:21
  748.8 17.8 %collective-permute-start.3 = (bf16[24,8,3072]{2,1,0:T(8,128)(2,1)}, bf16[24,8,3072]{2,1,0:T(8,128)(2,1)}, u32[]{:S(2)}, u32[]{:S(2)}) collective-permute-start(bf16[24,8,3072]{2,1,0:T(8,128)(2,1)} %get-tuple-element.8), channel_id=1, source_target_pairs={{8,0},{16,8},{24,16},{9,1},{17,9},{25,17},{10,2},{18,10},{26,18},{... | collective-permute-start | bytes 3538952 | tf_op jit(solution)/shard_map/ppermute | solution.py:22
  809.6 12.5 %copy-start.3 = (bf16[4,64,12,128]{3,2,1,0:T(8,128)(2,1)S(1)}, bf16[4,64,12,128]{3,2,1,0:T(8,128)(2,1)}, u32[]{:S(2)}) copy-start(bf16[4,64,12,128]{3,2,1,0:T(8,128)(2,1)} %reshape_reshape_reshape.6) | copy-start | bytes 2359300
  830.0 11.6 %copy-start.1 = (s32[8,16]{1,0:T(8,128)S(1)}, s32[8,16]{1,0:T(8,128)}, u32[]{:S(2)}) copy-start(s32[8,16]{1,0:T(8,128)} %param.13) | copy-start | bytes 1540
